TPU v7x, 256 devices: a whole 4x4x8 slice. The times are simulated.
256 devices in a mesh: dp: 32 (over y, z_hi, core), tensor: 8 (over z_lo, x).
Axes of the slice: x: 4, y: 4, z: 8 (z_hi: 4, z_lo: 2; z = z_hi * 2 + z_lo), core: 2. Of those that a mesh axis runs over, the one named last changes fastest.
Arguments:
- inputs: bfloat16 [32768, 2048], P(('dp', 'tensor')), may hold values from -6 to 6
- norm_gain: float32 [2048], replicated, may hold values from 0.1 to 1.9
- proj_weight: bfloat16 [2048, 3, 2048], P('dp', None, 'tensor'), may hold values from -0.125 to 0.125
- filters: float32 [3, 7, 2048], P(None, None, 'tensor'), may hold values from -2.4 to 2.4
- cotangent: bfloat16 [32768, 2048], P('dp', 'tensor'), may hold values from -18 to 18
Outputs:
- mixed: bfloat16 [32768, 2048], P('dp', 'tensor')
- grad_inputs: bfloat16 [32768, 2048], P(('dp', 'tensor'))
- grad_proj: bfloat16 [2048, 3, 2048], P('dp', None, 'tensor')
- grad_filters: float32 [3, 7, 2048], P(None, None, 'tensor')
- grad_gain: float32 [2048], replicated
All inputs are finite; a program needn't handle non-finite values.
Results may differ from a plain program's by a relative error of at most 0.02.
Values may be sent and summed in bfloat16 or wider, within the bound.
No kernel may reach another device: no remote copies, remote signals or barrier semaphores. Data moves between devices by JAX's collectives and lax.ppermute only.
A program may use at most 64 MiB of HBM per device.

v0:
```python
import jax
import jax.numpy as jnp
from jax import lax
from jax.sharding import PartitionSpec as P


def passed_along(shard, axis, by):
    size = lax.axis_size(axis)
    pairs = [(i, i + by) for i in range(size) if 0 <= i + by < size]
    return lax.ppermute(shard, axis, pairs)


def body(inputs, norm_gain, proj_weight, filters, cotangent):
    taps = filters.shape[1]
    width = taps - 1
    wide = inputs.astype(jnp.float32)
    inv_rms = lax.rsqrt(jnp.mean(wide * wide, axis=1, keepdims=True) + 1e-05)
    normed = (wide * inv_rms * norm_gain).astype(jnp.bfloat16)
    weights = lax.all_gather(proj_weight, "dp", axis=0, tiled=True)
    positions = lax.all_gather(normed, "tensor", axis=0, tiled=True)
    length = positions.shape[0]
    streams = jnp.einsum(
        "td,dsc->tsc", positions, weights, preferred_element_type=jnp.float32
    ).astype(jnp.bfloat16)
    before = passed_along(streams[length - width :], "dp", 1)
    extended = jnp.concatenate([before, streams], axis=0).astype(jnp.float32)
    conv = jnp.zeros(streams.shape, jnp.float32)
    for tap in range(taps):
        conv = conv + filters[:, tap, :] * extended[width - tap : width - tap + length]
    mixed = (conv[:, 0] * conv[:, 1] * conv[:, 2]).astype(jnp.bfloat16)
    grad_out = cotangent.astype(jnp.float32)
    grad_conv = jnp.stack(
        [
            grad_out * conv[:, 1] * conv[:, 2],
            grad_out * conv[:, 0] * conv[:, 2],
            grad_out * conv[:, 0] * conv[:, 1],
        ],
        axis=1,
    )
    after = passed_along(grad_conv[:width], "dp", -1)
    grad_extended = jnp.concatenate([grad_conv, after], axis=0)
    grad_acc = jnp.zeros(streams.shape, jnp.float32)
    for tap in range(taps):
        grad_acc = grad_acc + filters[:, tap, :] * grad_extended[tap : tap + length]
    grad_streams = grad_acc.astype(jnp.bfloat16)
    filter_local = jnp.stack(
        [
            jnp.sum(grad_conv * extended[width - tap : width - tap + length], axis=0)
            for tap in range(taps)
        ],
        axis=1,
    )
    normed_terms = jnp.einsum(
        "tsc,dsc->td", grad_streams, weights, preferred_element_type=jnp.float32
    )
    grad_normed = lax.psum_scatter(
        normed_terms.astype(jnp.bfloat16), "tensor", scatter_dimension=0, tiled=True
    ).astype(jnp.float32)
    weight_terms = jnp.einsum(
        "td,tsc->dsc", positions, grad_streams, preferred_element_type=jnp.float32
    )
    grad_proj = lax.psum_scatter(
        weight_terms.astype(jnp.bfloat16), "dp", scatter_dimension=0, tiled=True
    )
    scaled = norm_gain * grad_normed
    grad_inputs = inv_rms * (
        scaled - wide * inv_rms * inv_rms * jnp.mean(scaled * wide, axis=1, keepdims=True)
    )
    gain_local = jnp.sum(grad_normed * wide * inv_rms, axis=0)
    grad_filters = lax.psum(filter_local, "dp")
    grad_gain = lax.psum(gain_local, ("dp", "tensor"))
    return (mixed, grad_inputs.astype(jnp.bfloat16), grad_proj, grad_filters, grad_gain)


def solution(mesh):
    return jax.shard_map(
        body,
        mesh=mesh,
        in_specs=(
            P(("dp", "tensor"), None),
            P(),
            P("dp", None, "tensor"),
            P(None, None, "tensor"),
            P("dp", "tensor"),
        ),
        out_specs=(
            P("dp", "tensor"),
            P(("dp", "tensor"), None),
            P("dp", None, "tensor"),
            P(None, None, "tensor"),
            P(),
        ),
        check_vma=False,
    )
```

profile of v0, /device:TPU:10, one launch (start us, length us, event | category | flops | bytes accessed | tf_op | source)
XLA Modules:
  0.0 390.2 jit_solution(4973453960555978686)
XLA Ops:
  7.2 0.0 all-gather.5.cloned.1.call-start
  7.2 0.7 all-gather.5.cloned.1.call-update
  7.9 0.0 all-gather.3.cloned.1.call-start
  7.9 1.2 fusion.26
  9.2 2.0 fusion.20
  11.2 0.0 all-gather.3.cloned.1.call-update
  11.2 0.0 reduce-scatter.3.cloned.1.call-start
  11.3 1.0 fusion.30
  12.3 57.3 %all-gather.5.cloned.1.call-done = bf16[2048,3,256]{2,0,1:T(8,128)(2,1)} async-done(((bf16[64,3,256]{2,0,1:T(8,128)(2,1)}), bf16[2048,3,256]{2,0,1:T(8,128)(2,1)}) %all-gather.5.cloned.1.call-update) | async-done | bytes 3145744 | tf_op jit(solution)/shard_map/all_gather | solution.py:19
  69.6 54.1 %all-gather.3.cloned.1.call-done = bf16[1024,2048]{1,0:T(8,128)(2,1)} async-done(((bf16[128,2048]{1,0:T(8,128)(2,1)}), bf16[1024,2048]{1,0:T(8,128)(2,1)}) %all-gather.3.cloned.1.call-update) | async-done | bytes 4194320 | tf_op jit(solution)/shard_map/all_gather | solution.py:20
  123.8 6.6 %fusion.14 = bf16[1024,3,256]{2,0,1:T(8,128)(2,1)S(1)} fusion(bf16[2048,3,256]{2,0,1:T(8,128)(2,1)} %all-gather.5.cloned.1.call-done, bf16[1024,2048]{1,0:T(8,128)(2,1)} %all-gather.3.cloned.1.call-done), kind=kOutput, calls=%fused_computation.33 | convolution fusion | flops 3222011904 | bytes 8912896 | tf_op jit(solution)/shard_map/td,dsc->tsc/dot_general | solution.py:22
  130.4 1.9 collective-permute-start
  132.3 6.1 %collective-permute-done = bf16[6,3,256]{2,0,1:T(8,128)(2,1)S(1)} collective-permute-done((bf16[6,3,256]{2,0,1:T(8,128)(2,1)S(1)}, bf16[6,3,256]{2,0,1:T(8,128)(2,1)S(1)}, u32[]{:S(2)}, u32[]{:S(2)}) %collective-permute-start) | collective-permute-done | bytes 9248 | tf_op jit(solution)/shard_map/ppermute | solution.py:10
  138.4 0.3 maximum_convert_fusion
  138.7 0.0 copy-start.1
  138.7 2.6 multiply_add_fusion
  141.3 0.0 copy-done.1
  141.3 1.2 fusion.25
  142.5 2.9 multiply_reduce_fusion
  145.3 1.9 collective-permute-start.1
  147.3 1.5 collective-permute-done.1
  148.8 0.2 pad_maximum_fusion
  149.0 0.0 copy-start.3
  149.0 2.7 fusion.8
  151.7 0.0 copy-done.3
  151.7 5.1 %bitcast_convert_fusion = bf16[1024,2048]{1,0:T(8,128)(2,1)} fusion(bf16[1024,3,256]{2,0,1:T(8,128)(2,1)S(1)} %fusion.8, bf16[2048,3,256]{2,0,1:T(8,128)(2,1)S(1)} %copy-done.3), kind=kOutput, calls=%fused_computation | convolution fusion | flops 3223322624 | bytes 8912896 | tf_op jit(solution)/shard_map/tsc,dsc->td/dot_general | solution.py:53
  156.8 0.0 reduce-scatter.3.cloned.1.call-update
  156.8 0.2 reduce-scatter.5.cloned.1.call-start
  157.0 7.5 %fusion.4 = bf16[2048,3,256]{2,0,1:T(8,128)(2,1)} fusion(bf16[1024,3,256]{2,0,1:T(8,128)(2,1)S(1)} %fusion.8, bf16[1024,2048]{1,0:T(8,128)(2,1)} %all-gather.3.cloned.1.call-done), kind=kOutput, calls=%fused_computation.5 | convolution fusion | flops 3222798336 | bytes 8912896 | tf_op jit(solution)/shard_map/td,tsc->dsc/dot_general | solution.py:59
  164.6 0.0 copy-start
  164.6 0.0 copy-start.2
  164.6 0.0 reduce-scatter.5.cloned.1.call-update
  164.7 124.7 %psum.14 = f32[3,7,256]{2,0,1:T(4,128)S(1)} all-reduce(f32[3,7,256]{2,0,1:T(4,128)S(1)} %constant_dynamic-update-slice_fusion), channel_id=1, replica_groups=mesh['dp'=32,'tensor'=8] {'dp'}, use_global_device_ids=true, to_apply=%region_11.0 | all-reduce | flops 5376 | bytes 43008 | tf_op jit(solution)/shard_map/psum | solution.py:70
  289.3 0.6 copy.12
  290.0 0.0 reduce-scatter.3.cloned.1.call-done
  290.0 0.0 copy-done
  290.0 0.0 copy-done.2
  290.0 1.4 fusion.29
  291.3 90.1 %psum.15 = f32[2048]{0:T(1024)} all-reduce(f32[2048]{0:T(1024)S(1)} %get-tuple-element.17), channel_id=1, replica_groups=mesh['dp'=32,'tensor'=8] {'dp','tensor'}, use_global_device_ids=true, to_apply=%region_13.0 | all-reduce | flops 2048 | bytes 16384 | tf_op jit(solution)/shard_map/psum | solution.py:71
  381.5 2.2 fusion.23
  383.7 0.0 reduce-scatter.5.cloned.1.call-done
  (15 shorter events, 0.1 us)
Async XLA Ops:
  7.2 62.5 %all-gather.5.cloned.1.call-start = ((), (), s32[]{:S(2)}) async-start(), calls=%async_computation.3 | async-start | bytes 3244032 | tf_op jit(solution)/shard_map/all_gather | solution.py:19
  7.9 115.9 %all-gather.3.cloned.1.call-start = ((), (), s32[]{:S(2)}) async-start(), calls=%async_computation.2 | async-start | bytes 4718592 | tf_op jit(solution)/shard_map/all_gather | solution.py:20
  11.2 278.7 %reduce-scatter.3.cloned.1.call-start = ((), (), s32[]{:S(2)}) async-start(), calls=%async_computation.4 | async-start | bytes 4718592 | tf_op jit(solution)/shard_map/reduce_scatter | solution.py:56
  130.4 8.0 %collective-permute-start = (bf16[6,3,256]{2,0,1:T(8,128)(2,1)S(1)}, bf16[6,3,256]{2,0,1:T(8,128)(2,1)S(1)}, u32[]{:S(2)}, u32[]{:S(2)}) collective-permute-start(bf16[6,3,256]{2,0,1:T(8,128)(2,1)S(1)} %slice.120), channel_id=1, source_target_pairs={{0,8},{8,16},{16,24},{24,32},{32,40},{40,48},{48,56},{56,64},{64,7... | collective-permute-start | bytes 27656 | tf_op jit(solution)/shard_map/ppermute | solution.py:10
  138.7 2.6 copy-start.1
  145.3 3.4 collective-permute-start.1
  149.0 2.7 copy-start.3
  156.8 226.9 %reduce-scatter.5.cloned.1.call-start = ((), (), s32[]{:S(2)}) async-start(), calls=%async_computation.5 | async-start | bytes 3244032 | tf_op jit(solution)/shard_map/reduce_scatter | solution.py:62
  164.6 125.4 %copy-start = (bf16[128,2048]{1,0:T(8,128)(2,1)S(1)}, bf16[128,2048]{1,0:T(8,128)(2,1)}, u32[]{:S(2)}) copy-start(bf16[128,2048]{1,0:T(8,128)(2,1)} %param.5) | copy-start | bytes 1572868
  164.6 125.4 %copy-start.2 = (f32[2048]{0:T(1024)S(1)}, f32[2048]{0:T(1024)}, u32[]{:S(2)}) copy-start(f32[2048]{0:T(1024)} %param.6) | copy-start | bytes 24580
Sparse Core Ops, SparseCore 0:
  10.7 58.9 all-gather.4
  72.0 51.7 all-gather.2
  156.9 54.7 reduce-scatter.2
  216.1 96.0 reduce-scatter.4
where the time goes:
time: 394 us; the launch traced here: 390 us
  blocking collectives  215 us (55%)
  waiting for transfers between devices  120 us (30%)
  matrix products  19.2 us (5%)
  other arithmetic  16.6 us (4%)
  between operations  13.9 us (4%)
  starting transfers between devices  4.18 us (1%)
    psum x1, blocking collectives, body(): grad_filters = lax.psum(filter_local, 'dp')  125 us
    psum x1, blocking collectives, body(): grad_gain = lax.psum(gain_local, ('dp', 'tensor'))  90.1 us
    all_gather x1, waiting for transfers between devices, body(): weights = lax.all_gather(proj_weight, 'dp', axis=0, tiled=True)  57.3 us
    all_gather x1, waiting for transfers between devices, body(): positions = lax.all_gather(normed, 'tensor', axis=0, tiled=True)  54.1 us
  transfers between devices with their start and end apart: 6, of which 4 were waited for; matrix products, arithmetic and copies ran while one was open for 4% of the time, Pallas kernels for 0%

commit v1 on v0

--- a/solution.py
+++ b/solution.py
@@ -10,14 +10,28 @@
     return lax.ppermute(shard, axis, pairs)
 
 
+def butterfly_sum(value, axis):
+    size = lax.axis_size(axis)
+    step = 1
+    while step < size:
+        pairs = [(i, i ^ step) for i in range(size)]
+        value = value + lax.ppermute(value, axis, pairs)
+        step *= 2
+    return value
+
+
 def body(inputs, norm_gain, proj_weight, filters, cotangent):
     taps = filters.shape[1]
     width = taps - 1
+    rows = inputs.shape[0]
     wide = inputs.astype(jnp.float32)
     inv_rms = lax.rsqrt(jnp.mean(wide * wide, axis=1, keepdims=True) + 1e-05)
-    normed = (wide * inv_rms * norm_gain).astype(jnp.bfloat16)
     weights = lax.all_gather(proj_weight, "dp", axis=0, tiled=True)
-    positions = lax.all_gather(normed, "tensor", axis=0, tiled=True)
+    gathered = lax.all_gather(inputs, "tensor", axis=0, tiled=True)
+    wide_all = gathered.astype(jnp.float32)
+    inv_all = lax.rsqrt(jnp.mean(wide_all * wide_all, axis=1, keepdims=True) + 1e-05)
+    unit_all = wide_all * inv_all
+    positions = (unit_all * norm_gain).astype(jnp.bfloat16)
     length = positions.shape[0]
     streams = jnp.einsum(
         "td,dsc->tsc", positions, weights, preferred_element_type=jnp.float32
@@ -50,11 +64,13 @@
         ],
         axis=1,
     )
+    grad_filters = butterfly_sum(filter_local, "dp")
     normed_terms = jnp.einsum(
         "tsc,dsc->td", grad_streams, weights, preferred_element_type=jnp.float32
-    )
+    ).astype(jnp.bfloat16)
+    gain_local = jnp.sum(normed_terms.astype(jnp.float32) * unit_all, axis=0)
     grad_normed = lax.psum_scatter(
-        normed_terms.astype(jnp.bfloat16), "tensor", scatter_dimension=0, tiled=True
+        normed_terms, "tensor", scatter_dimension=0, tiled=True
     ).astype(jnp.float32)
     weight_terms = jnp.einsum(
         "td,tsc->dsc", positions, grad_streams, preferred_element_type=jnp.float32
@@ -62,13 +78,11 @@
     grad_proj = lax.psum_scatter(
         weight_terms.astype(jnp.bfloat16), "dp", scatter_dimension=0, tiled=True
     )
+    grad_gain = butterfly_sum(butterfly_sum(gain_local, "dp"), "tensor")
     scaled = norm_gain * grad_normed
     grad_inputs = inv_rms * (
         scaled - wide * inv_rms * inv_rms * jnp.mean(scaled * wide, axis=1, keepdims=True)
     )
-    gain_local = jnp.sum(grad_normed * wide * inv_rms, axis=0)
-    grad_filters = lax.psum(filter_local, "dp")
-    grad_gain = lax.psum(gain_local, ("dp", "tensor"))
     return (mixed, grad_inputs.astype(jnp.bfloat16), grad_proj, grad_filters, grad_gain)
 
 

time: 394 us -> 323 us (0.82)
  blocking collectives: 215 us -> 0 us
  waiting for transfers between devices: 120 us -> 247 us
  starting transfers between devices: 4.18 us -> 21.4 us
    psum x2 -> x0, blocking collectives: 215 us -> none  [the longest x1 125 us: body(): grad_filters = lax.psum(filter_local, 'dp')]
    reduce_scatter x1, waiting for transfers between devices: 0.01 us -> 95.8 us  [body(): lax.psum_scatter(weight_terms.astype(jnp.bfloat16), 'dp', scatter_dimensi...]
    ppermute x0 -> x13, waiting for transfers between devices: none -> 28.1 us  [butterfly_sum(): value = value + lax.ppermute(value, axis, pairs)]
    ppermute x0 -> x13, starting transfers between devices: none -> 17 us  [butterfly_sum(): value = value + lax.ppermute(value, axis, pairs)]
  transfers between devices with their start and end apart: 6 -> 19, of which waited for: 4 -> 15; matrix products, arithmetic and copies ran while one was open for 4% -> 5% of each run, Pallas kernels for 0% -> 0%
where the time goes in v1:
time: 323 us; the launch traced here: 322 us
  waiting for transfers between devices  247 us (76%)
  starting transfers between devices  21.4 us (7%)
  matrix products  19.7 us (6%)
  other arithmetic  17.1 us (5%)
  between operations  14 us (4%)
    reduce_scatter x1, waiting for transfers between devices, body(): lax.psum_scatter(weight_terms.astype(jnp.bfloat16), 'dp', scatter_dimensi...  95.8 us
    all_gather x1, waiting for transfers between devices, body(): weights = lax.all_gather(proj_weight, 'dp', axis=0, tiled=True)  56.7 us
    all_gather x1, waiting for transfers between devices, body(): gathered = lax.all_gather(inputs, 'tensor', axis=0, tiled=True)  55.9 us
    ppermute x13, waiting for transfers between devices, butterfly_sum(): value = value + lax.ppermute(value, axis, pairs)  28.1 us
    ppermute x13, starting transfers between devices, butterfly_sum(): value = value + lax.ppermute(value, axis, pairs)  17 us
    dot_general x1, matrix products, body(): jnp.einsum('td,tsc->dsc', positions, grad_streams, preferred_element_type...  7.86 us
    ppermute x2, waiting for transfers between devices, passed_along(): return lax.ppermute(shard, axis, pairs)  7.45 us
    dot_general x1, matrix products, body(): jnp.einsum('td,dsc->tsc', positions, weights, preferred_element_type=jnp....  6.64 us
  transfers between devices with their start and end apart: 19, of which 15 were waited for; matrix products, arithmetic and copies ran while one was open for 5% of the time, Pallas kernels for 0%

profile of v1, /device:TPU:10, one launch (start us, length us, event | category | flops | bytes accessed | tf_op | source)
XLA Modules:
  0.0 321.5 jit_solution(6911648904704494626)
XLA Ops:
  7.2 0.0 copy-start.3
  7.2 0.0 all-gather.3.cloned.1.call-start
  7.2 0.7 all-gather.3.cloned.1.call-update
  7.9 0.0 all-gather.5.cloned.1.call-start
  8.0 0.7 all-gather.5.cloned.1.call-update
  8.7 0.0 reduce-scatter.3.cloned.1.call-start
  8.7 1.0 fusion.28
  9.8 55.9 %all-gather.3.cloned.1.call-done = bf16[1024,2048]{1,0:T(8,128)(2,1)} async-done(((bf16[128,2048]{1,0:T(8,128)(2,1)}), bf16[1024,2048]{1,0:T(8,128)(2,1)}) %all-gather.3.cloned.1.call-update) | async-done | bytes 4194320 | tf_op jit(solution)/shard_map/all_gather | solution.py:30
  65.6 3.1 fusion.4
  68.7 56.7 %all-gather.5.cloned.1.call-done = bf16[2048,3,256]{2,0,1:T(8,128)(2,1)} async-done(((bf16[64,3,256]{2,0,1:T(8,128)(2,1)}), bf16[2048,3,256]{2,0,1:T(8,128)(2,1)}) %all-gather.5.cloned.1.call-update) | async-done | bytes 3145744 | tf_op jit(solution)/shard_map/all_gather | solution.py:29
  125.4 0.0 copy-done.3
  125.4 6.6 %fusion.16 = bf16[1024,3,256]{2,0,1:T(8,128)(2,1)S(1)} fusion(bf16[2048,3,256]{2,0,1:T(8,128)(2,1)} %all-gather.5.cloned.1.call-done, bf16[1024,2048]{1,0:T(8,128)(2,1)} %all-gather.3.cloned.1.call-done, f32[2048]{0:T(1024)S(1)} %copy-done.3, f32[1024]{0:T(1024)S(1)} %add_rsqrt_fusion), kind=kOutput, calls=%fused_computation.34 | convolution fusion | flops 3230400512 | bytes 8925184 | tf_op jit(solution)/shard_map/td,dsc->tsc/dot_general | solution.py:36
  132.1 2.2 collective-permute-start
  134.3 6.0 %collective-permute-done = bf16[6,3,256]{2,0,1:T(8,128)(2,1)S(1)} collective-permute-done((bf16[6,3,256]{2,0,1:T(8,128)(2,1)S(1)}, bf16[6,3,256]{2,0,1:T(8,128)(2,1)S(1)}, u32[]{:S(2)}, u32[]{:S(2)}) %collective-permute-start) | collective-permute-done | bytes 9248 | tf_op jit(solution)/shard_map/ppermute | solution.py:10
  140.2 0.3 maximum_convert_fusion
  140.5 0.0 copy-start.2
  140.5 2.6 multiply_add_fusion
  143.1 0.0 copy-done.2
  143.1 1.1 fusion.20
  144.3 2.9 multiply_reduce_fusion
  147.2 1.9 collective-permute-start.1
  149.1 1.5 collective-permute-done.1
  150.6 0.2 pad_maximum_fusion
  150.8 0.0 copy-start.1
  150.8 0.0 copy-start.4
  150.8 2.7 fusion.7
  153.5 0.4 copy-done.4
  154.0 5.2 %fusion.3 = (f32[2048]{0:T(1024)S(1)}, bf16[1024,2048]{1,0:T(8,128)(2,1)}) fusion(bf16[1024,2048]{1,0:T(8,128)(2,1)S(1)} %copy-done.1, f32[1024]{0:T(1024)S(1)} %add_rsqrt_fusion, bf16[1024,3,256]{2,0,1:T(8,128)(2,1)S(1)} %fusion.7, bf16[2048,3,256]{2,0,1:T(8,128)(2,1)S(1)} %copy-done.4), kind=kOutput, calls=%fused_computation.5 | convolution fusion | flops 3233806336 | bytes 13119488 | tf_op jit(solution)/shard_map/tsc,dsc->td/dot_general | solution.py:68
  159.2 0.0 reduce-scatter.3.cloned.1.call-update
  159.2 0.2 reduce-scatter.5.cloned.1.call-start
  159.4 7.9 %convolution_convert_fusion = bf16[2048,3,256]{2,0,1:T(8,128)(2,1)} fusion(bf16[1024,3,256]{2,0,1:T(8,128)(2,1)S(1)} %fusion.7, bf16[1024,2048]{1,0:T(8,128)(2,1)} %all-gather.3.cloned.1.call-done, f32[2048]{0:T(1024)S(1)} %copy-done.3, f32[1024]{0:T(1024)S(1)} %add_rsqrt_fusion), kind=kOutput, calls=%fused_computation.9 | convolution fusion | flops 3231186944 | bytes 8925184 | tf_op jit(solution)/shard_map/td,tsc->dsc/dot_general | solution.py:75
  167.3 0.0 reduce-scatter.5.cloned.1.call-update
  167.4 0.1 collective-permute-start.2
  167.5 1.2 collective-permute-done.2
  168.7 1.1 collective-permute-start.3
  169.8 0.1 collective-permute-start.7
  169.8 3.7 %collective-permute-done.3 = f32[3,7,256]{2,0,1:T(4,128)S(1)} collective-permute-done((f32[3,7,256]{2,0,1:T(4,128)S(1)}, f32[3,7,256]{2,0,1:T(4,128)S(1)}, u32[]{:S(2)}, u32[]{:S(2)}) %collective-permute-start.3) | collective-permute-done | bytes 21536 | tf_op jit(solution)/shard_map/ppermute | solution.py:18
  173.6 4.2 %collective-permute-start.4 = (f32[3,7,256]{2,0,1:T(4,128)S(1)}, f32[3,7,256]{2,0,1:T(4,128)S(1)}, u32[]{:S(2)}, u32[]{:S(2)}) collective-permute-start(f32[3,7,256]{2,0,1:T(4,128)S(1)} %add.118), channel_id=1, source_target_pairs={{0,32},{8,40},{16,48},{24,56},{32,0},{40,8},{48,16},{56,24},{64,96... | collective-permute-start | bytes 64520 | tf_op jit(solution)/shard_map/ppermute | solution.py:18
  177.8 0.0 collective-permute-done.7
  177.8 3.0 collective-permute-start.8
  180.8 2.2 collective-permute-done.8
  183.0 1.3 collective-permute-start.9
  184.3 0.0 collective-permute-done.4
  184.3 1.2 collective-permute-start.5
  185.5 5.1 %collective-permute-done.9 = f32[2048]{0:T(1024)S(1)} collective-permute-done((f32[2048]{0:T(1024)S(1)}, f32[2048]{0:T(1024)S(1)}, u32[]{:S(2)}, u32[]{:S(2)}) %collective-permute-start.9) | collective-permute-done | bytes 8224 | tf_op jit(solution)/shard_map/ppermute | solution.py:18
  190.6 0.2 collective-permute-start.10
  190.8 3.4 %collective-permute-done.10 = f32[2048]{0:T(1024)S(1)} collective-permute-done((f32[2048]{0:T(1024)S(1)}, f32[2048]{0:T(1024)S(1)}, u32[]{:S(2)}, u32[]{:S(2)}) %collective-permute-start.10) | collective-permute-done | bytes 8224 | tf_op jit(solution)/shard_map/ppermute | solution.py:18
  194.2 0.5 collective-permute-start.11
  194.7 4.7 %collective-permute-done.11 = f32[2048]{0:T(1024)S(1)} collective-permute-done((f32[2048]{0:T(1024)S(1)}, f32[2048]{0:T(1024)S(1)}, u32[]{:S(2)}, u32[]{:S(2)}) %collective-permute-start.11) | collective-permute-done | bytes 8224 | tf_op jit(solution)/shard_map/ppermute | solution.py:18
  199.4 0.5 collective-permute-start.12
  199.9 0.0 collective-permute-done.5
  199.9 1.0 collective-permute-start.6
  201.0 2.4 collective-permute-done.12
  203.4 2.3 collective-permute-start.13
  205.7 3.2 collective-permute-done.13
  208.9 1.5 collective-permute-start.14
  210.4 2.2 collective-permute-done.14
  212.6 0.6 add.129
  213.2 0.0 collective-permute-done.6
  213.2 0.6 copy.12
  213.8 1.8 reduce-scatter.3.cloned.1.call-done
  215.6 1.4 fusion.21
  217.0 2.2 fusion.26
  219.1 95.8 %reduce-scatter.5.cloned.1.call-done = bf16[64,3,256]{2,0,1:T(8,128)(2,1)} async-done(((bf16[2048,3,256]{2,0,1:T(8,128)(2,1)}), bf16[64,3,256]{2,0,1:T(8,128)(2,1)}) %reduce-scatter.5.cloned.1.call-update) | async-done | bytes 98320 | tf_op jit(solution)/shard_map/reduce_scatter | solution.py:78
  (31 shorter events, 0.2 us)
Async XLA Ops:
  7.2 118.2 %copy-start.3 = (f32[2048]{0:T(1024)S(1)}, f32[2048]{0:T(1024)}, u32[]{:S(2)}) copy-start(f32[2048]{0:T(1024)} %param.6) | copy-start | bytes 24580
  7.2 58.5 %all-gather.3.cloned.1.call-start = ((), (), s32[]{:S(2)}) async-start(), calls=%async_computation.2 | async-start | bytes 4718592 | tf_op jit(solution)/shard_map/all_gather | solution.py:30
  7.9 117.5 %all-gather.5.cloned.1.call-start = ((), (), s32[]{:S(2)}) async-start(), calls=%async_computation.3 | async-start | bytes 3244032 | tf_op jit(solution)/shard_map/all_gather | solution.py:29
  8.7 206.9 %reduce-scatter.3.cloned.1.call-start = ((), (), s32[]{:S(2)}) async-start(), calls=%async_computation.4 | async-start | bytes 4718592 | tf_op jit(solution)/shard_map/reduce_scatter | solution.py:72
  132.1 8.2 %collective-permute-start = (bf16[6,3,256]{2,0,1:T(8,128)(2,1)S(1)}, bf16[6,3,256]{2,0,1:T(8,128)(2,1)S(1)}, u32[]{:S(2)}, u32[]{:S(2)}) collective-permute-start(bf16[6,3,256]{2,0,1:T(8,128)(2,1)S(1)} %slice.120), channel_id=1, source_target_pairs={{0,8},{8,16},{16,24},{24,32},{32,40},{40,48},{48,56},{56,64},{64,7... | collective-permute-start | bytes 27656 | tf_op jit(solution)/shard_map/ppermute | solution.py:10
  140.5 2.6 copy-start.2
  147.2 3.4 %collective-permute-start.1 = (f32[6,3,256]{2,0,1:T(8,128)S(1)}, f32[6,3,256]{2,0,1:T(8,128)S(1)}, u32[]{:S(2)}, u32[]{:S(2)}) collective-permute-start(f32[6,3,256]{2,0,1:T(8,128)S(1)} %slice.131), channel_id=1, source_target_pairs={{8,0},{16,8},{24,16},{32,24},{40,32},{48,40},{56,48},{64,56},{72,6... | collective-permute-start | bytes 55304 | tf_op jit(solution)/shard_map/ppermute | solution.py:10
  150.8 2.7 copy-start.1
  150.8 3.2 copy-start.4
  159.2 155.8 %reduce-scatter.5.cloned.1.call-start = ((), (), s32[]{:S(2)}) async-start(), calls=%async_computation.5 | async-start | bytes 3244032 | tf_op jit(solution)/shard_map/reduce_scatter | solution.py:78
  167.3 48.3 %copy-start = (bf16[128,2048]{1,0:T(8,128)(2,1)S(1)}, bf16[128,2048]{1,0:T(8,128)(2,1)}, u32[]{:S(2)}) copy-start(bf16[128,2048]{1,0:T(8,128)(2,1)} %param.5) | copy-start | bytes 1572868
  167.4 1.3 collective-permute-start.2
  168.7 4.9 %collective-permute-start.3 = (f32[3,7,256]{2,0,1:T(4,128)S(1)}, f32[3,7,256]{2,0,1:T(4,128)S(1)}, u32[]{:S(2)}, u32[]{:S(2)}) collective-permute-start(f32[3,7,256]{2,0,1:T(4,128)S(1)} %add.117), channel_id=1, source_target_pairs={{0,16},{8,24},{16,0},{24,8},{32,48},{40,56},{48,32},{56,40},{64,80... | collective-permute-start | bytes 64520 | tf_op jit(solution)/shard_map/ppermute | solution.py:18
  169.8 8.0 %collective-permute-start.7 = (f32[2048]{0:T(1024)S(1)}, f32[2048]{0:T(1024)S(1)}, u32[]{:S(2)}, u32[]{:S(2)}) collective-permute-start(f32[2048]{0:T(1024)S(1)} %get-tuple-element.34), channel_id=1, source_target_pairs={{0,8},{8,0},{16,24},{24,16},{32,40},{40,32},{48,56},{56,48},{64,72... | collective-permute-start | bytes 24584 | tf_op jit(solution)/shard_map/ppermute | solution.py:18
  173.6 10.7 %collective-permute-start.4 = (f32[3,7,256]{2,0,1:T(4,128)S(1)}, f32[3,7,256]{2,0,1:T(4,128)S(1)}, u32[]{:S(2)}, u32[]{:S(2)}) collective-permute-start(f32[3,7,256]{2,0,1:T(4,128)S(1)} %add.118), channel_id=1, source_target_pairs={{0,32},{8,40},{16,48},{24,56},{32,0},{40,8},{48,16},{56,24},{64,96... | collective-permute-start | bytes 64520 | tf_op jit(solution)/shard_map/ppermute | solution.py:18
  177.8 5.2 %collective-permute-start.8 = (f32[2048]{0:T(1024)S(1)}, f32[2048]{0:T(1024)S(1)}, u32[]{:S(2)}, u32[]{:S(2)}) collective-permute-start(f32[2048]{0:T(1024)S(1)} %add.122), channel_id=1, source_target_pairs={{0,16},{8,24},{16,0},{24,8},{32,48},{40,56},{48,32},{56,40},{64,80... | collective-permute-start | bytes 24584 | tf_op jit(solution)/shard_map/ppermute | solution.py:18
  183.0 7.6 %collective-permute-start.9 = (f32[2048]{0:T(1024)S(1)}, f32[2048]{0:T(1024)S(1)}, u32[]{:S(2)}, u32[]{:S(2)}) collective-permute-start(f32[2048]{0:T(1024)S(1)} %add.123), channel_id=1, source_target_pairs={{0,32},{8,40},{16,48},{24,56},{32,0},{40,8},{48,16},{56,24},{64,96... | collective-permute-start | bytes 24584 | tf_op jit(solution)/shard_map/ppermute | solution.py:18
  184.3 15.6 %collective-permute-start.5 = (f32[3,7,256]{2,0,1:T(4,128)S(1)}, f32[3,7,256]{2,0,1:T(4,128)S(1)}, u32[]{:S(2)}, u32[]{:S(2)}) collective-permute-start(f32[3,7,256]{2,0,1:T(4,128)S(1)} %add.119), channel_id=1, source_target_pairs={{0,64},{8,72},{16,80},{24,88},{32,96},{40,104},{48,112},{56,120},{... | collective-permute-start | bytes 64520 | tf_op jit(solution)/shard_map/ppermute | solution.py:18
  190.6 3.7 %collective-permute-start.10 = (f32[2048]{0:T(1024)S(1)}, f32[2048]{0:T(1024)S(1)}, u32[]{:S(2)}, u32[]{:S(2)}) collective-permute-start(f32[2048]{0:T(1024)S(1)} %add.124), channel_id=1, source_target_pairs={{0,64},{8,72},{16,80},{24,88},{32,96},{40,104},{48,112},{56,120},{... | collective-permute-start | bytes 24584 | tf_op jit(solution)/shard_map/ppermute | solution.py:18
  194.2 5.2 %collective-permute-start.11 = (f32[2048]{0:T(1024)S(1)}, f32[2048]{0:T(1024)S(1)}, u32[]{:S(2)}, u32[]{:S(2)}) collective-permute-start(f32[2048]{0:T(1024)S(1)} %add.125), channel_id=1, source_target_pairs={{0,128},{8,136},{16,144},{24,152},{32,160},{40,168},{48,176},{56,1... | collective-permute-start | bytes 24584 | tf_op jit(solution)/shard_map/ppermute | solution.py:18
  199.4 4.0 %collective-permute-start.12 = (f32[2048]{0:T(1024)S(1)}, f32[2048]{0:T(1024)S(1)}, u32[]{:S(2)}, u32[]{:S(2)}) collective-permute-start(f32[2048]{0:T(1024)S(1)} %add.126), channel_id=1, source_target_pairs={{0,1},{1,0},{2,3},{3,2},{4,5},{5,4},{6,7},{7,6},{8,9},{9,8},{10,11... | collective-permute-start | bytes 24584 | tf_op jit(solution)/shard_map/ppermute | solution.py:18
  199.9 13.2 %collective-permute-start.6 = (f32[3,7,256]{2,0,1:T(4,128)S(1)}, f32[3,7,256]{2,0,1:T(4,128)S(1)}, u32[]{:S(2)}, u32[]{:S(2)}) collective-permute-start(f32[3,7,256]{2,0,1:T(4,128)S(1)} %add.120), channel_id=1, source_target_pairs={{0,128},{8,136},{16,144},{24,152},{32,160},{40,168},{48,176},{56,1... | collective-permute-start | bytes 64520 | tf_op jit(solution)/shard_map/ppermute | solution.py:18
  203.4 5.5 %collective-permute-start.13 = (f32[2048]{0:T(1024)S(1)}, f32[2048]{0:T(1024)S(1)}, u32[]{:S(2)}, u32[]{:S(2)}) collective-permute-start(f32[2048]{0:T(1024)S(1)} %add.127), channel_id=1, source_target_pairs={{0,2},{1,3},{2,0},{3,1},{4,6},{5,7},{6,4},{7,5},{8,10},{9,11},{10,... | collective-permute-start | bytes 24584 | tf_op jit(solution)/shard_map/ppermute | solution.py:18
  208.9 3.7 %collective-permute-start.14 = (f32[2048]{0:T(1024)S(1)}, f32[2048]{0:T(1024)S(1)}, u32[]{:S(2)}, u32[]{:S(2)}) collective-permute-start(f32[2048]{0:T(1024)S(1)} %add.128), channel_id=1, source_target_pairs={{0,4},{1,5},{2,6},{3,7},{4,0},{5,1},{6,2},{7,3},{8,12},{9,13},{10,... | collective-permute-start | bytes 24584 | tf_op jit(solution)/shard_map/ppermute | solution.py:18
Sparse Core Ops, SparseCore 0:
  9.8 55.7 all-gather.2
  68.3 57.0 all-gather.4
  159.3 56.1 reduce-scatter.2
  219.9 95.0 reduce-scatter.4

commit v2 on v1

--- a/solution.py
+++ b/solution.py
@@ -2,6 +2,8 @@
 import jax.numpy as jnp
 from jax import lax
 from jax.sharding import PartitionSpec as P
+
+RING = 4
 
 
 def passed_along(shard, axis, by):
@@ -20,22 +22,87 @@
     return value
 
 
+def along_x(value, by):
+    size = lax.axis_size("tensor")
+    pairs = [(i, (i // RING) * RING + (i % RING + by) % RING) for i in range(size)]
+    return lax.ppermute(value, "tensor", pairs)
+
+
+def across_z(value):
+    size = lax.axis_size("tensor")
+    pairs = [(i, (i + RING) % size) for i in range(size)]
+    return lax.ppermute(value, "tensor", pairs)
+
+
+def relative_slots():
+    me = lax.axis_index("tensor")
+    z, x = me // RING, me % RING
+    r = jnp.arange(2 * RING, dtype=jnp.int32)
+    dz, dx = r // RING, r % RING
+    absolute = ((z + dz) % 2) * RING + (x + dx) % RING
+    zs, xs = r // RING, r % RING
+    relative = ((zs + z) % 2) * RING + (xs - x) % RING
+    return absolute, relative
+
+
+def gather_tensor(own):
+    half = own.shape[0] // 2
+    partner = across_z(own)
+    from_left = along_x(own, 1)
+    from_right = along_x(own, -1)
+    partner_left = along_x(partner, 1)
+    partner_right = along_x(partner, -1)
+    far = jnp.concatenate(
+        [along_x(from_left[:half], 1), along_x(from_right[half:], -1)], axis=0
+    )
+    partner_far = jnp.concatenate(
+        [along_x(partner_left[:half], 1), along_x(partner_right[half:], -1)], axis=0
+    )
+    return jnp.stack(
+        [own, from_right, far, from_left, partner, partner_right, partner_far, partner_left]
+    )
+
+
+def scatter_tensor(blocks):
+    half = blocks.shape[1] // 2
+    wide = blocks.astype(jnp.float32)
+    shard = [wide[dx :: RING] for dx in range(RING)]
+    got_left = along_x(blocks[2::RING, :half], 1)
+    got_right = along_x(blocks[2::RING, half:], -1)
+    send_right = jnp.concatenate(
+        [shard[1][:, :half] + got_left.astype(jnp.float32), shard[1][:, half:]], axis=1
+    )
+    send_left = jnp.concatenate(
+        [shard[3][:, :half], shard[3][:, half:] + got_right.astype(jnp.float32)], axis=1
+    )
+    column = (
+        shard[0]
+        + along_x(send_right.astype(jnp.bfloat16), 1).astype(jnp.float32)
+        + along_x(send_left.astype(jnp.bfloat16), -1).astype(jnp.float32)
+    )
+    return column[0] + across_z(column[1].astype(jnp.bfloat16)).astype(jnp.float32)
+
+
 def body(inputs, norm_gain, proj_weight, filters, cotangent):
     taps = filters.shape[1]
     width = taps - 1
     rows = inputs.shape[0]
+    absolute, relative = relative_slots()
     wide = inputs.astype(jnp.float32)
     inv_rms = lax.rsqrt(jnp.mean(wide * wide, axis=1, keepdims=True) + 1e-05)
     weights = lax.all_gather(proj_weight, "dp", axis=0, tiled=True)
-    gathered = lax.all_gather(inputs, "tensor", axis=0, tiled=True)
+    gathered = gather_tensor(inputs).reshape(-1, inputs.shape[1])
     wide_all = gathered.astype(jnp.float32)
     inv_all = lax.rsqrt(jnp.mean(wide_all * wide_all, axis=1, keepdims=True) + 1e-05)
     unit_all = wide_all * inv_all
     positions = (unit_all * norm_gain).astype(jnp.bfloat16)
     length = positions.shape[0]
-    streams = jnp.einsum(
+    streams_rel = jnp.einsum(
         "td,dsc->tsc", positions, weights, preferred_element_type=jnp.float32
     ).astype(jnp.bfloat16)
+    streams = jnp.take(
+        streams_rel.reshape((-1, rows) + streams_rel.shape[1:]), relative, axis=0
+    ).reshape(streams_rel.shape)
     before = passed_along(streams[length - width :], "dp", 1)
     extended = jnp.concatenate([before, streams], axis=0).astype(jnp.float32)
     conv = jnp.zeros(streams.shape, jnp.float32)
@@ -56,7 +123,10 @@
     grad_acc = jnp.zeros(streams.shape, jnp.float32)
     for tap in range(taps):
         grad_acc = grad_acc + filters[:, tap, :] * grad_extended[tap : tap + length]
-    grad_streams = grad_acc.astype(jnp.bfloat16)
+    grad_streams_abs = grad_acc.astype(jnp.bfloat16)
+    grad_streams = jnp.take(
+        grad_streams_abs.reshape((-1, rows) + grad_streams_abs.shape[1:]), absolute, axis=0
+    ).reshape(grad_streams_abs.shape)
     filter_local = jnp.stack(
         [
             jnp.sum(grad_conv * extended[width - tap : width - tap + length], axis=0)
@@ -69,9 +139,7 @@
         "tsc,dsc->td", grad_streams, weights, preferred_element_type=jnp.float32
     ).astype(jnp.bfloat16)
     gain_local = jnp.sum(normed_terms.astype(jnp.float32) * unit_all, axis=0)
-    grad_normed = lax.psum_scatter(
-        normed_terms, "tensor", scatter_dimension=0, tiled=True
-    ).astype(jnp.float32)
+    grad_normed = scatter_tensor(normed_terms.reshape(-1, rows, normed_terms.shape[1]))
     weight_terms = jnp.einsum(
         "td,tsc->dsc", positions, grad_streams, preferred_element_type=jnp.float32
     )

time: 323 us -> 229 us (0.71)
  waiting for transfers between devices: 247 us -> 121 us
  starting transfers between devices: 21.4 us -> 46.4 us
  local copies, waits for them, and re-layouts: 2.17 us -> 8.35 us
    reduce_scatter x1, waiting for transfers between devices: 95.8 us -> 0.01 us  [body(): lax.psum_scatter(weight_terms.astype(jnp.bfloat16), 'dp', scatter_dimensi...]
    ppermute x0 -> x14, waiting for transfers between devices: none -> 58.9 us  [the longest x12 58.9 us: along_x(): return lax.ppermute(value, 'tensor', pairs)]
    all_gather x1 -> x0, waiting for transfers between devices: 55.9 us -> none  [body(): gathered = lax.all_gather(inputs, 'tensor', axis=0, tiled=True)]
    all_gather x1, waiting for transfers between devices: 56.7 us -> 14.6 us  [body(): weights = lax.all_gather(proj_weight, 'dp', axis=0, tiled=True)]
    ppermute x0 -> x14, starting transfers between devices: none -> 19.9 us  [the longest x12 16.1 us: along_x(): return lax.ppermute(value, 'tensor', pairs)]
    ppermute x13, waiting for transfers between devices: 28.1 us -> 39.2 us  [butterfly_sum(): value = value + lax.ppermute(value, axis, pairs)]
    ppermute x13, starting transfers between devices: 17 us -> 22.1 us  [butterfly_sum(): value = value + lax.ppermute(value, axis, pairs)]
    convert_element_type x1 -> x3, other arithmetic: 2.7 us -> 6.77 us  [the longest x1 3.01 us: body(): positions = (unit_all * norm_gain).astype(jnp.bfloat16)]
  transfers between devices with their start and end apart: 19 -> 31, of which waited for: 15 -> 20; matrix products, arithmetic and copies ran while one was open for 5% -> 8% of each run, Pallas kernels for 0% -> 0%
where the time goes in v2:
time: 229 us; the launch traced here: 226 us
  waiting for transfers between devices  121 us (53%)
  starting transfers between devices  46.4 us (20%)
  other arithmetic  18.5 us (8%)
  matrix products  18.2 us (8%)
  between operations  14.5 us (6%)
  local copies, waits for them, and re-layouts  8.35 us (4%)
    ppermute x12, waiting for transfers between devices, along_x(): return lax.ppermute(value, 'tensor', pairs)  58.9 us
    ppermute x13, waiting for transfers between devices, butterfly_sum(): value = value + lax.ppermute(value, axis, pairs)  39.2 us
    ppermute x13, starting transfers between devices, butterfly_sum(): value = value + lax.ppermute(value, axis, pairs)  22.1 us
    ppermute x12, starting transfers between devices, along_x(): return lax.ppermute(value, 'tensor', pairs)  16.1 us
    all_gather x1, waiting for transfers between devices, body(): weights = lax.all_gather(proj_weight, 'dp', axis=0, tiled=True)  14.6 us
    ppermute x2, waiting for transfers between devices, passed_along(): return lax.ppermute(shard, axis, pairs)  7.2 us
    dot_general x1, matrix products, body(): jnp.einsum('td,dsc->tsc', positions, weights, preferred_element_type=jnp....  6.57 us
    dot_general x1, matrix products, body(): jnp.einsum('tsc,dsc->td', grad_streams, weights, preferred_element_type=j...  6.26 us
  transfers between devices with their start and end apart: 31, of which 20 were waited for; matrix products, arithmetic and copies ran while one was open for 8% of the time, Pallas kernels for 0%

profile of v2, /device:TPU:10, one launch (start us, length us, event | category | flops | bytes accessed | tf_op | source)
XLA Modules:
  0.0 226.5 jit_solution(14906287461013129139)
XLA Ops:
  7.2 0.7 all-gather.2.cloned.1.call-update
  7.9 0.6 collective-permute-start
  8.6 1.5 collective-permute-start.1
  10.0 1.9 collective-permute-start.4
  12.0 1.0 fusion.45
  13.1 1.1 bitcast_dynamic-update-slice_fusion.5
  14.1 9.1 %collective-permute-done.1 = bf16[128,2048]{1,0:T(8,128)(2,1)S(1)} collective-permute-done((bf16[128,2048]{1,0:T(8,128)(2,1)}, bf16[128,2048]{1,0:T(8,128)(2,1)S(1)}, u32[]{:S(2)}, u32[]{:S(2)}) %collective-permute-start.1) | collective-permute-done | bytes 524320 | tf_op jit(solution)/shard_map/ppermute | solution.py:28
  23.2 0.5 collective-permute-start.2
  23.8 2.6 %collective-permute-start.3 = (bf16[64,2048]{1,0:T(8,128)(2,1)S(1)}, bf16[64,2048]{1,0:T(8,128)(2,1)S(1)}, u32[]{:S(2)}, u32[]{:S(2)}) collective-permute-start(bf16[64,2048]{1,0:T(8,128)(2,1)S(1)} %slice.188), channel_id=1, source_target_pairs={{0,3},{1,0},{2,1},{3,2},{4,7},{5,4},{6,5},{7,6},{8,11},{9,8},{10,9... | collective-permute-start | bytes 786440 | tf_op jit(solution)/shard_map/ppermute | solution.py:28
  26.4 3.2 %collective-permute-start.5 = (bf16[128,2048]{1,0:T(8,128)(2,1)S(1)}, bf16[128,2048]{1,0:T(8,128)(2,1)S(1)}, u32[]{:S(2)}, u32[]{:S(2)}) collective-permute-start(bf16[128,2048]{1,0:T(8,128)(2,1)S(1)} %collective-permute-done.4), channel_id=1, source_target_pairs={{0,3},{1,0},{2,1},{3,2},{4,7},{5,4},{6,5},{7,6},{8,11},{9,8},{10,9... | collective-permute-start | bytes 1572872 | tf_op jit(solution)/shard_map/ppermute | solution.py:28
  29.6 3.0 %collective-permute-done.2 = bf16[64,2048]{1,0:T(8,128)(2,1)S(1)} collective-permute-done((bf16[64,2048]{1,0:T(8,128)(2,1)S(1)}, bf16[64,2048]{1,0:T(8,128)(2,1)S(1)}, u32[]{:S(2)}, u32[]{:S(2)}) %collective-permute-start.2) | collective-permute-done | bytes 262176 | tf_op jit(solution)/shard_map/ppermute | solution.py:28
  32.6 0.5 collective-permute-done.3
  33.2 9.3 %collective-permute-done.6 = bf16[128,2048]{1,0:T(8,128)(2,1)S(1)} collective-permute-done((bf16[128,2048]{1,0:T(8,128)(2,1)S(1)}, bf16[128,2048]{1,0:T(8,128)(2,1)S(1)}, u32[]{:S(2)}, u32[]{:S(2)}) %collective-permute-start.6) | collective-permute-done | bytes 524320 | tf_op jit(solution)/shard_map/ppermute | solution.py:28
  42.7 3.2 %collective-permute-start.8 = (bf16[64,2048]{1,0:T(8,128)(2,1)S(1)}, bf16[64,2048]{1,0:T(8,128)(2,1)S(1)}, u32[]{:S(2)}, u32[]{:S(2)}) collective-permute-start(bf16[64,2048]{1,0:T(8,128)(2,1)S(1)} %slice.190), channel_id=1, source_target_pairs={{0,3},{1,0},{2,1},{3,2},{4,7},{5,4},{6,5},{7,6},{8,11},{9,8},{10,9... | collective-permute-start | bytes 786440 | tf_op jit(solution)/shard_map/ppermute | solution.py:28
  46.0 4.0 %collective-permute-done.7 = bf16[64,2048]{1,0:T(8,128)(2,1)S(1)} collective-permute-done((bf16[64,2048]{1,0:T(8,128)(2,1)S(1)}, bf16[64,2048]{1,0:T(8,128)(2,1)S(1)}, u32[]{:S(2)}, u32[]{:S(2)}) %collective-permute-start.7) | collective-permute-done | bytes 262176 | tf_op jit(solution)/shard_map/ppermute | solution.py:28
  50.1 0.9 multiply_reduce_fusion.1
  51.0 1.1 copy-done
  52.0 3.0 %multiply_convert_fusion.1 = bf16[1024,2048]{1,0:T(8,128)(2,1)} fusion(bf16[8,128,2048]{2,1,0:T(8,128)(2,1)S(1)} %bitcast_dynamic-update-slice_fusion, f32[2048]{0:T(1024)S(1)} %copy-done.4, f32[1024]{0:T(1024)S(1)} %get-tuple-element.49), kind=kLoop, calls=%fused_computation.6 | loop fusion | flops 8388608 | bytes 8400896 | tf_op jit(solution)/shard_map/convert_element_type | solution.py:98
  55.1 14.6 %all-gather.2.cloned.1.call-done = bf16[2048,3,256]{2,0,1:T(8,128)(2,1)} async-done(((bf16[64,3,256]{2,0,1:T(8,128)(2,1)}), bf16[2048,3,256]{2,0,1:T(8,128)(2,1)}) %all-gather.2.cloned.1.call-update) | async-done | bytes 3145744 | tf_op jit(solution)/shard_map/all_gather | solution.py:93
  69.6 6.6 %fusion.16 = bf16[1024,3,256]{2,0,1:T(8,128)(2,1)S(1)} fusion(bf16[2048,3,256]{2,0,1:T(8,128)(2,1)} %all-gather.2.cloned.1.call-done, bf16[1024,2048]{1,0:T(8,128)(2,1)} %multiply_convert_fusion.1), kind=kOutput, calls=%fused_computation.39 | convolution fusion | flops 3222011904 | bytes 8912896 | tf_op jit(solution)/shard_map/td,dsc->tsc/dot_general | solution.py:100
  76.2 0.6 gather_fusion
  77.2 2.2 collective-permute-start.9
  79.4 5.9 %collective-permute-done.9 = bf16[6,3,256]{2,0,1:T(8,128)(2,1)S(1)} collective-permute-done((bf16[6,3,256]{2,0,1:T(8,128)(2,1)S(1)}, bf16[6,3,256]{2,0,1:T(8,128)(2,1)S(1)}, u32[]{:S(2)}, u32[]{:S(2)}) %collective-permute-start.9) | collective-permute-done | bytes 9248 | tf_op jit(solution)/shard_map/ppermute | solution.py:12
  85.7 2.6 %multiply_add_fusion = f32[1024,3,256]{2,0,1:T(8,128)S(1)} fusion(f32[1030,3,256]{2,0,1:T(8,128)S(1)} %maximum_convert_fusion, f32[3,256]{1,0:T(4,128)S(1)} %get-tuple-element.52, f32[3,256]{1,0:T(4,128)S(1)} %get-tuple-element.53, f32[3,256]{1,0:T(4,128)S(1)} %get-tuple-element.54, f32[3,256]{1,0:T(4,128)S(1)} %get-tuple-element.55, ...), kind=kLoop, calls=%fused_computation.37 | loop fusion | flops 10223616 | bytes 25187328 | tf_op jit(solution)/shard_map/add | solution.py:110
  88.3 1.2 fusion.20
  89.5 2.9 %multiply_reduce_fusion.2 = (f32[3,256]{1,0:T(4,128)S(1)}, f32[3,256]{1,0:T(4,128)S(1)}, f32[3,256]{1,0:T(4,128)S(1)}, f32[3,256]{1,0:T(4,128)S(1)}, f32[3,256]{...) fusion(f32[1030,3,256]{2,0,1:T(8,128)S(1)} %maximum_convert_fusion, ...), kind=kLoop, calls=%fused_computation.30 | loop fusion | flops 12577536 | bytes 28333056 | tf_op jit(solution)/shard_map/reduce_sum | solution.py:132
  92.3 2.1 collective-permute-start.10
  94.5 1.3 collective-permute-done.10
  96.0 2.7 %fusion.10 = bf16[1024,3,256]{2,0,1:T(8,128)(2,1)S(1)} fusion(f32[1030,3,256]{2,0,1:T(8,128)S(1)} %pad_maximum_fusion, f32[3,256]{1,0:T(4,128)S(1)} %get-tuple-element.52, f32[3,256]{1,0:T(4,128)S(1)} %get-tuple-element.53, f32[3,256]{1,0:T(4,128)S(1)} %get-tuple-element.54, f32[3,256]{1,0:T(4,128)S(1)} %get-tuple-element.55, ...), kind=kLoop, calls=%fused_computation.18 | loop fusion | flops 12582912 | bytes 23614464 | tf_op jit(solution)/shard_map/convert_element_type | solution.py:126
  98.8 0.6 gather_fusion.1
  99.8 1.8 copy-done.1
  101.6 5.3 %bitcast_convert_fusion.1 = bf16[2048,3,256]{2,0,1:T(8,128)(2,1)} fusion(bf16[8,128,3,256]{3,1,2,0:T(8,128)(2,1)S(1)} %broadcast_select_fusion, bf16[8,128,2048]{2,1,0:T(8,128)(2,1)S(1)} %copy-done.1, f32[2048]{0:T(1024)S(1)} %copy-done.4, f32[8,128]{1,0:T(8,128)S(1)} %get-tuple-element.48), kind=kOutput, calls=%fused_computation.8 | convolution fusion | flops 3231186944 | bytes 8925184 | tf_op jit(solution)/shard_map/td,tsc->dsc/dot_general | solution.py:143
  107.0 6.3 %multiply_reduce_fusion = (f32[2048]{0:T(1024)S(1)}, bf16[1024,2048]{1,0:T(8,128)(2,1)S(1)}) fusion(bf16[8,128,2048]{2,1,0:T(8,128)(2,1)} %copy-done, f32[1024]{0:T(1024)S(1)} %get-tuple-element.49, bf16[1024,3,256]{2,0,1:T(8,128)(2,1)S(1)} %bitcast.136, bf16[2048,3,256]{2,0,1:T(8,128)(2,1)} %all-gather.2.cloned.1.call-done), kind=kOutput, calls=%fused_computation.4 | convolution fusion | flops 3233806336 | bytes 13119488 | tf_op jit(solution)/shard_map/tsc,dsc->td/dot_general | solution.py:138
  113.3 1.5 collective-permute-start.11
  114.9 0.5 fusion.44
  115.5 0.6 collective-permute-start.13
  116.2 10.9 %collective-permute-done.11 = bf16[2,64,2048]{2,1,0:T(8,128)(2,1)S(1)} collective-permute-done((bf16[2,64,2048]{2,1,0:T(8,128)(2,1)S(1)}, bf16[2,64,2048]{2,1,0:T(8,128)(2,1)S(1)}, u32[]{:S(2)}, u32[]{:S(2)}) %collective-permute-start.11) | collective-permute-done | bytes 524320 | tf_op jit(solution)/shard_map/ppermute | solution.py:28
  127.3 1.5 collective-permute-start.12
  129.2 0.6 collective-permute-start.14
  129.8 1.1 convert_element_type.81
  130.9 20.5 %collective-permute-done.12 = bf16[2,128,2048]{2,1,0:T(8,128)(2,1)S(1)} collective-permute-done((bf16[2,128,2048]{2,1,0:T(8,128)(2,1)S(1)}, bf16[2,128,2048]{2,1,0:T(8,128)(2,1)S(1)}, u32[]{:S(2)}, u32[]{:S(2)}) %collective-permute-start.12) | collective-permute-done | bytes 1048608 | tf_op jit(solution)/shard_map/ppermute | solution.py:28
  151.5 1.5 collective-permute-done.14
  153.0 0.5 convert_add_fusion
  153.5 1.9 collective-permute-start.15
  155.4 1.2 collective-permute-done.16
  156.6 0.7 collective-permute-start.17
  157.4 21.0 %collective-permute-done.17 = f32[3,7,256]{2,0,1:T(4,128)S(1)} collective-permute-done((f32[3,7,256]{2,0,1:T(4,128)S(1)}, f32[3,7,256]{2,0,1:T(4,128)S(1)}, u32[]{:S(2)}, u32[]{:S(2)}) %collective-permute-start.17) | collective-permute-done | bytes 21536 | tf_op jit(solution)/shard_map/ppermute | solution.py:20
  178.4 4.0 %collective-permute-start.18 = (f32[3,7,256]{2,0,1:T(4,128)S(1)}, f32[3,7,256]{2,0,1:T(4,128)S(1)}, u32[]{:S(2)}, u32[]{:S(2)}) collective-permute-start(f32[3,7,256]{2,0,1:T(4,128)S(1)} %add.199), channel_id=1, source_target_pairs={{0,32},{8,40},{16,48},{24,56},{32,0},{40,8},{48,16},{56,24},{64,96... | collective-permute-start | bytes 64520 | tf_op jit(solution)/shard_map/ppermute | solution.py:20
  182.4 3.4 %collective-permute-start.22 = (f32[2048]{0:T(1024)S(1)}, f32[2048]{0:T(1024)S(1)}, u32[]{:S(2)}, u32[]{:S(2)}) collective-permute-start(f32[2048]{0:T(1024)S(1)} %add.203), channel_id=1, source_target_pairs={{0,16},{8,24},{16,0},{24,8},{32,48},{40,56},{48,32},{56,40},{64,80... | collective-permute-start | bytes 24584 | tf_op jit(solution)/shard_map/ppermute | solution.py:20
  185.9 1.7 collective-permute-done.22
  187.5 2.3 %collective-permute-start.23 = (f32[2048]{0:T(1024)S(1)}, f32[2048]{0:T(1024)S(1)}, u32[]{:S(2)}, u32[]{:S(2)}) collective-permute-start(f32[2048]{0:T(1024)S(1)} %add.204), channel_id=1, source_target_pairs={{0,32},{8,40},{16,48},{24,56},{32,0},{40,8},{48,16},{56,24},{64,96... | collective-permute-start | bytes 24584 | tf_op jit(solution)/shard_map/ppermute | solution.py:20
  190.0 5.1 %collective-permute-done.23 = f32[2048]{0:T(1024)S(1)} collective-permute-done((f32[2048]{0:T(1024)S(1)}, f32[2048]{0:T(1024)S(1)}, u32[]{:S(2)}, u32[]{:S(2)}) %collective-permute-start.23) | collective-permute-done | bytes 8224 | tf_op jit(solution)/shard_map/ppermute | solution.py:20
  195.1 2.0 collective-permute-start.24
  197.1 1.6 collective-permute-done.24
  198.8 1.9 collective-permute-start.25
  200.7 3.3 %collective-permute-done.25 = f32[2048]{0:T(1024)S(1)} collective-permute-done((f32[2048]{0:T(1024)S(1)}, f32[2048]{0:T(1024)S(1)}, u32[]{:S(2)}, u32[]{:S(2)}) %collective-permute-start.25) | collective-permute-done | bytes 8224 | tf_op jit(solution)/shard_map/ppermute | solution.py:20
  204.0 1.7 collective-permute-start.26
  205.6 2.2 collective-permute-start.20
  207.8 3.7 %collective-permute-start.27 = (f32[2048]{0:T(1024)S(1)}, f32[2048]{0:T(1024)S(1)}, u32[]{:S(2)}, u32[]{:S(2)}) collective-permute-start(f32[2048]{0:T(1024)S(1)} %add.208), channel_id=1, source_target_pairs={{0,2},{1,3},{2,0},{3,1},{4,6},{5,7},{6,4},{7,5},{8,10},{9,11},{10,... | collective-permute-start | bytes 24584 | tf_op jit(solution)/shard_map/ppermute | solution.py:20
  211.5 1.6 collective-permute-done.27
  213.2 3.6 %collective-permute-done.28 = f32[2048]{0:T(1024)S(1)} collective-permute-done((f32[2048]{0:T(1024)S(1)}, f32[2048]{0:T(1024)S(1)}, u32[]{:S(2)}, u32[]{:S(2)}) %collective-permute-start.28) | collective-permute-done | bytes 8224 | tf_op jit(solution)/shard_map/ppermute | solution.py:20
  216.8 0.6 add.210
  217.4 0.6 copy.21
  218.5 1.2 fusion.26
  (88 shorter events, 3.3 us)
Async XLA Ops:
  7.2 62.5 %all-gather.2.cloned.1.call-start = ((), (), s32[]{:S(2)}) async-start(), calls=%async_computation.1 | async-start | bytes 3244032 | tf_op jit(solution)/shard_map/all_gather | solution.py:93
  7.9 211.7 %reduce-scatter.2.cloned.1.call-start = ((), (), s32[]{:S(2)}) async-start(), calls=%async_computation.2 | async-start | bytes 3244032 | tf_op jit(solution)/shard_map/reduce_scatter | solution.py:146
  7.9 15.8 %collective-permute-start = (bf16[128,2048]{1,0:T(8,128)(2,1)}, bf16[128,2048]{1,0:T(8,128)(2,1)S(1)}, u32[]{:S(2)}, u32[]{:S(2)}) collective-permute-start(bf16[128,2048]{1,0:T(8,128)(2,1)} %param.7), channel_id=1, source_target_pairs={{0,3},{1,0},{2,1},{3,2},{4,7},{5,4},{6,5},{7,6},{8,11},{9,8},{10,9... | collective-permute-start | bytes 1572872 | tf_op jit(solution)/shard_map/ppermute | solution.py:28
  8.6 14.6 %collective-permute-start.1 = (bf16[128,2048]{1,0:T(8,128)(2,1)}, bf16[128,2048]{1,0:T(8,128)(2,1)S(1)}, u32[]{:S(2)}, u32[]{:S(2)}) collective-permute-start(bf16[128,2048]{1,0:T(8,128)(2,1)} %param.7), channel_id=1, source_target_pairs={{0,1},{1,2},{2,3},{3,0},{4,5},{5,6},{6,7},{7,4},{8,9},{9,10},{10,1... | collective-permute-start | bytes 1572872 | tf_op jit(solution)/shard_map/ppermute | solution.py:28
  10.0 16.3 %collective-permute-start.4 = (bf16[128,2048]{1,0:T(8,128)(2,1)}, bf16[128,2048]{1,0:T(8,128)(2,1)S(1)}, u32[]{:S(2)}, u32[]{:S(2)}) collective-permute-start(bf16[128,2048]{1,0:T(8,128)(2,1)} %param.7), channel_id=1, source_target_pairs={{0,4},{1,5},{2,6},{3,7},{4,0},{5,1},{6,2},{7,3},{8,12},{9,13},{10,... | collective-permute-start | bytes 1572872 | tf_op jit(solution)/shard_map/ppermute | solution.py:34
  23.2 9.4 %collective-permute-start.2 = (bf16[64,2048]{1,0:T(8,128)(2,1)S(1)}, bf16[64,2048]{1,0:T(8,128)(2,1)S(1)}, u32[]{:S(2)}, u32[]{:S(2)}) collective-permute-start(bf16[64,2048]{1,0:T(8,128)(2,1)S(1)} %slice.187), channel_id=1, source_target_pairs={{0,1},{1,2},{2,3},{3,0},{4,5},{5,6},{6,7},{7,4},{8,9},{9,10},{10,1... | collective-permute-start | bytes 786440 | tf_op jit(solution)/shard_map/ppermute | solution.py:28
  23.8 9.3 %collective-permute-start.3 = (bf16[64,2048]{1,0:T(8,128)(2,1)S(1)}, bf16[64,2048]{1,0:T(8,128)(2,1)S(1)}, u32[]{:S(2)}, u32[]{:S(2)}) collective-permute-start(bf16[64,2048]{1,0:T(8,128)(2,1)S(1)} %slice.188), channel_id=1, source_target_pairs={{0,3},{1,0},{2,1},{3,2},{4,7},{5,4},{6,5},{7,6},{8,11},{9,8},{10,9... | collective-permute-start | bytes 786440 | tf_op jit(solution)/shard_map/ppermute | solution.py:28
  26.4 16.3 %collective-permute-start.5 = (bf16[128,2048]{1,0:T(8,128)(2,1)S(1)}, bf16[128,2048]{1,0:T(8,128)(2,1)S(1)}, u32[]{:S(2)}, u32[]{:S(2)}) collective-permute-start(bf16[128,2048]{1,0:T(8,128)(2,1)S(1)} %collective-permute-done.4), channel_id=1, source_target_pairs={{0,3},{1,0},{2,1},{3,2},{4,7},{5,4},{6,5},{7,6},{8,11},{9,8},{10,9... | collective-permute-start | bytes 1572872 | tf_op jit(solution)/shard_map/ppermute | solution.py:28
  29.6 13.0 %collective-permute-start.6 = (bf16[128,2048]{1,0:T(8,128)(2,1)S(1)}, bf16[128,2048]{1,0:T(8,128)(2,1)S(1)}, u32[]{:S(2)}, u32[]{:S(2)}) collective-permute-start(bf16[128,2048]{1,0:T(8,128)(2,1)S(1)} %collective-permute-done.4), channel_id=1, source_target_pairs={{0,1},{1,2},{2,3},{3,0},{4,5},{5,6},{6,7},{7,4},{8,9},{9,10},{10,1... | collective-permute-start | bytes 1572872 | tf_op jit(solution)/shard_map/ppermute | solution.py:28
  42.6 7.4 %collective-permute-start.7 = (bf16[64,2048]{1,0:T(8,128)(2,1)S(1)}, bf16[64,2048]{1,0:T(8,128)(2,1)S(1)}, u32[]{:S(2)}, u32[]{:S(2)}) collective-permute-start(bf16[64,2048]{1,0:T(8,128)(2,1)S(1)} %slice.189), channel_id=1, source_target_pairs={{0,1},{1,2},{2,3},{3,0},{4,5},{5,6},{6,7},{7,4},{8,9},{9,10},{10,1... | collective-permute-start | bytes 786440 | tf_op jit(solution)/shard_map/ppermute | solution.py:28
  42.7 7.3 %collective-permute-start.8 = (bf16[64,2048]{1,0:T(8,128)(2,1)S(1)}, bf16[64,2048]{1,0:T(8,128)(2,1)S(1)}, u32[]{:S(2)}, u32[]{:S(2)}) collective-permute-start(bf16[64,2048]{1,0:T(8,128)(2,1)S(1)} %slice.190), channel_id=1, source_target_pairs={{0,3},{1,0},{2,1},{3,2},{4,7},{5,4},{6,5},{7,6},{8,11},{9,8},{10,9... | collective-permute-start | bytes 786440 | tf_op jit(solution)/shard_map/ppermute | solution.py:28
  46.0 6.1 %copy-start.4 = (f32[2048]{0:T(1024)S(1)}, f32[2048]{0:T(1024)}, u32[]{:S(2)}) copy-start(f32[2048]{0:T(1024)} %param.8) | copy-start | bytes 24580
  50.1 2.0 copy-start
  77.2 8.2 %collective-permute-start.9 = (bf16[6,3,256]{2,0,1:T(8,128)(2,1)S(1)}, bf16[6,3,256]{2,0,1:T(8,128)(2,1)S(1)}, u32[]{:S(2)}, u32[]{:S(2)}) collective-permute-start(bf16[6,3,256]{2,0,1:T(8,128)(2,1)S(1)} %slice.191), channel_id=1, source_target_pairs={{0,8},{8,16},{16,24},{24,32},{32,40},{40,48},{48,56},{56,64},{64,7... | collective-permute-start | bytes 27656 | tf_op jit(solution)/shard_map/ppermute | solution.py:12
  85.7 2.6 %copy-start.3 = (bf16[1024,256]{1,0:T(8,128)(2,1)S(1)}, bf16[1024,256]{1,0:T(8,128)(2,1)}, u32[]{:S(2)}) copy-start(bf16[1024,256]{1,0:T(8,128)(2,1)} %param.11) | copy-start | bytes 1572868
  92.3 3.4 %collective-permute-start.10 = (f32[6,3,256]{2,0,1:T(8,128)S(1)}, f32[6,3,256]{2,0,1:T(8,128)S(1)}, u32[]{:S(2)}, u32[]{:S(2)}) collective-permute-start(f32[6,3,256]{2,0,1:T(8,128)S(1)} %slice.202), channel_id=1, source_target_pairs={{8,0},{16,8},{24,16},{32,24},{40,32},{48,40},{56,48},{64,56},{72,6... | collective-permute-start | bytes 55304 | tf_op jit(solution)/shard_map/ppermute | solution.py:12
  99.5 2.2 copy-start.1
  113.3 13.7 %collective-permute-start.11 = (bf16[2,64,2048]{2,1,0:T(8,128)(2,1)S(1)}, bf16[2,64,2048]{2,1,0:T(8,128)(2,1)S(1)}, u32[]{:S(2)}, u32[]{:S(2)}) collective-permute-start(bf16[2,64,2048]{2,1,0:T(8,128)(2,1)S(1)} %get-tuple-element.32), channel_id=1, source_target_pairs={{0,1},{1,2},{2,3},{3,0},{4,5},{5,6},{6,7},{7,4},{8,9},{9,10},{10,1... | collective-permute-start | bytes 1572872 | tf_op jit(solution)/shard_map/ppermute | solution.py:28
  115.5 13.5 %collective-permute-start.13 = (bf16[2,64,2048]{2,1,0:T(8,128)(2,1)S(1)}, bf16[2,64,2048]{2,1,0:T(8,128)(2,1)S(1)}, u32[]{:S(2)}, u32[]{:S(2)}) collective-permute-start(bf16[2,64,2048]{2,1,0:T(8,128)(2,1)S(1)} %get-tuple-element.33), channel_id=1, source_target_pairs={{0,3},{1,0},{2,1},{3,2},{4,7},{5,4},{6,5},{7,6},{8,11},{9,8},{10,9... | collective-permute-start | bytes 1572872 | tf_op jit(solution)/shard_map/ppermute | solution.py:28
  127.3 24.1 %collective-permute-start.12 = (bf16[2,128,2048]{2,1,0:T(8,128)(2,1)S(1)}, bf16[2,128,2048]{2,1,0:T(8,128)(2,1)S(1)}, u32[]{:S(2)}, u32[]{:S(2)}) collective-permute-start(bf16[2,128,2048]{2,1,0:T(8,128)(2,1)S(1)} %pad_maximum_fusion.2), channel_id=1, source_target_pairs={{0,1},{1,2},{2,3},{3,0},{4,5},{5,6},{6,7},{7,4},{8,9},{9,10},{10,1... | collective-permute-start | bytes 3145736 | tf_op jit(solution)/shard_map/ppermute | solution.py:28
  129.2 23.8 %collective-permute-start.14 = (bf16[2,128,2048]{2,1,0:T(8,128)(2,1)S(1)}, bf16[2,128,2048]{2,1,0:T(8,128)(2,1)S(1)}, u32[]{:S(2)}, u32[]{:S(2)}) collective-permute-start(bf16[2,128,2048]{2,1,0:T(8,128)(2,1)S(1)} %pad_maximum_fusion.3), channel_id=1, source_target_pairs={{0,3},{1,0},{2,1},{3,2},{4,7},{5,4},{6,5},{7,6},{8,11},{9,8},{10,9... | collective-permute-start | bytes 3145736 | tf_op jit(solution)/shard_map/ppermute | solution.py:28
  130.9 87.2 %copy-start.2 = (bf16[128,2048]{1,0:T(8,128)(2,1)S(1)}, bf16[128,2048]{1,0:T(8,128)(2,1)}, u32[]{:S(2)}) copy-start(bf16[128,2048]{1,0:T(8,128)(2,1)} %param.7) | copy-start | bytes 1572868
  153.5 64.6 %collective-permute-start.15 = (bf16[128,2048]{1,0:T(8,128)(2,1)S(1)}, bf16[128,2048]{1,0:T(8,128)(2,1)S(1)}, u32[]{:S(2)}, u32[]{:S(2)}) collective-permute-start(bf16[128,2048]{1,0:T(8,128)(2,1)S(1)} %fusion.32), channel_id=1, source_target_pairs={{0,4},{1,5},{2,6},{3,7},{4,0},{5,1},{6,2},{7,3},{8,12},{9,13},{10,... | collective-permute-start | bytes 1572872 | tf_op jit(solution)/shard_map/ppermute | solution.py:34
  155.4 1.2 collective-permute-start.16
  156.6 21.7 %collective-permute-start.17 = (f32[3,7,256]{2,0,1:T(4,128)S(1)}, f32[3,7,256]{2,0,1:T(4,128)S(1)}, u32[]{:S(2)}, u32[]{:S(2)}) collective-permute-start(f32[3,7,256]{2,0,1:T(4,128)S(1)} %add.198), channel_id=1, source_target_pairs={{0,16},{8,24},{16,0},{24,8},{32,48},{40,56},{48,32},{56,40},{64,80... | collective-permute-start | bytes 64520 | tf_op jit(solution)/shard_map/ppermute | solution.py:20
  157.4 25.1 %collective-permute-start.21 = (f32[2048]{0:T(1024)S(1)}, f32[2048]{0:T(1024)S(1)}, u32[]{:S(2)}, u32[]{:S(2)}) collective-permute-start(f32[2048]{0:T(1024)S(1)} %get-tuple-element.50), channel_id=1, source_target_pairs={{0,8},{8,0},{16,24},{24,16},{32,40},{40,32},{48,56},{56,48},{64,72... | collective-permute-start | bytes 24584 | tf_op jit(solution)/shard_map/ppermute | solution.py:20
  178.4 11.5 %collective-permute-start.18 = (f32[3,7,256]{2,0,1:T(4,128)S(1)}, f32[3,7,256]{2,0,1:T(4,128)S(1)}, u32[]{:S(2)}, u32[]{:S(2)}) collective-permute-start(f32[3,7,256]{2,0,1:T(4,128)S(1)} %add.199), channel_id=1, source_target_pairs={{0,32},{8,40},{16,48},{24,56},{32,0},{40,8},{48,16},{56,24},{64,96... | collective-permute-start | bytes 64520 | tf_op jit(solution)/shard_map/ppermute | solution.py:20
  182.4 5.1 %collective-permute-start.22 = (f32[2048]{0:T(1024)S(1)}, f32[2048]{0:T(1024)S(1)}, u32[]{:S(2)}, u32[]{:S(2)}) collective-permute-start(f32[2048]{0:T(1024)S(1)} %add.203), channel_id=1, source_target_pairs={{0,16},{8,24},{16,0},{24,8},{32,48},{40,56},{48,32},{56,40},{64,80... | collective-permute-start | bytes 24584 | tf_op jit(solution)/shard_map/ppermute | solution.py:20
  187.5 7.6 %collective-permute-start.23 = (f32[2048]{0:T(1024)S(1)}, f32[2048]{0:T(1024)S(1)}, u32[]{:S(2)}, u32[]{:S(2)}) collective-permute-start(f32[2048]{0:T(1024)S(1)} %add.204), channel_id=1, source_target_pairs={{0,32},{8,40},{16,48},{24,56},{32,0},{40,8},{48,16},{56,24},{64,96... | collective-permute-start | bytes 24584 | tf_op jit(solution)/shard_map/ppermute | solution.py:20
  189.9 15.7 %collective-permute-start.19 = (f32[3,7,256]{2,0,1:T(4,128)S(1)}, f32[3,7,256]{2,0,1:T(4,128)S(1)}, u32[]{:S(2)}, u32[]{:S(2)}) collective-permute-start(f32[3,7,256]{2,0,1:T(4,128)S(1)} %add.200), channel_id=1, source_target_pairs={{0,64},{8,72},{16,80},{24,88},{32,96},{40,104},{48,112},{56,120},{... | collective-permute-start | bytes 64520 | tf_op jit(solution)/shard_map/ppermute | solution.py:20
  195.1 3.7 %collective-permute-start.24 = (f32[2048]{0:T(1024)S(1)}, f32[2048]{0:T(1024)S(1)}, u32[]{:S(2)}, u32[]{:S(2)}) collective-permute-start(f32[2048]{0:T(1024)S(1)} %add.205), channel_id=1, source_target_pairs={{0,64},{8,72},{16,80},{24,88},{32,96},{40,104},{48,112},{56,120},{... | collective-permute-start | bytes 24584 | tf_op jit(solution)/shard_map/ppermute | solution.py:20
  198.8 5.2 %collective-permute-start.25 = (f32[2048]{0:T(1024)S(1)}, f32[2048]{0:T(1024)S(1)}, u32[]{:S(2)}, u32[]{:S(2)}) collective-permute-start(f32[2048]{0:T(1024)S(1)} %add.206), channel_id=1, source_target_pairs={{0,128},{8,136},{16,144},{24,152},{32,160},{40,168},{48,176},{56,1... | collective-permute-start | bytes 24584 | tf_op jit(solution)/shard_map/ppermute | solution.py:20
  204.0 3.9 %collective-permute-start.26 = (f32[2048]{0:T(1024)S(1)}, f32[2048]{0:T(1024)S(1)}, u32[]{:S(2)}, u32[]{:S(2)}) collective-permute-start(f32[2048]{0:T(1024)S(1)} %add.207), channel_id=1, source_target_pairs={{0,1},{1,0},{2,3},{3,2},{4,5},{5,4},{6,7},{7,6},{8,9},{9,8},{10,11... | collective-permute-start | bytes 24584 | tf_op jit(solution)/shard_map/ppermute | solution.py:20
  205.6 11.8 %collective-permute-start.20 = (f32[3,7,256]{2,0,1:T(4,128)S(1)}, f32[3,7,256]{2,0,1:T(4,128)S(1)}, u32[]{:S(2)}, u32[]{:S(2)}) collective-permute-start(f32[3,7,256]{2,0,1:T(4,128)S(1)} %add.201), channel_id=1, source_target_pairs={{0,128},{8,136},{16,144},{24,152},{32,160},{40,168},{48,176},{56,1... | collective-permute-start | bytes 64520 | tf_op jit(solution)/shard_map/ppermute | solution.py:20
  207.8 5.4 %collective-permute-start.27 = (f32[2048]{0:T(1024)S(1)}, f32[2048]{0:T(1024)S(1)}, u32[]{:S(2)}, u32[]{:S(2)}) collective-permute-start(f32[2048]{0:T(1024)S(1)} %add.208), channel_id=1, source_target_pairs={{0,2},{1,3},{2,0},{3,1},{4,6},{5,7},{6,4},{7,5},{8,10},{9,11},{10,... | collective-permute-start | bytes 24584 | tf_op jit(solution)/shard_map/ppermute | solution.py:20
  213.2 3.7 %collective-permute-start.28 = (f32[2048]{0:T(1024)S(1)}, f32[2048]{0:T(1024)S(1)}, u32[]{:S(2)}, u32[]{:S(2)}) collective-permute-start(f32[2048]{0:T(1024)S(1)} %add.209), channel_id=1, source_target_pairs={{0,4},{1,5},{2,6},{3,7},{4,0},{5,1},{6,2},{7,3},{8,12},{9,13},{10,... | collective-permute-start | bytes 24584 | tf_op jit(solution)/shard_map/ppermute | solution.py:20
Sparse Core Ops, SparseCore 0:
  10.7 58.9 all-gather.1
  107.1 99.0 reduce-scatter.1
